TPU v7x, 32 devices: a whole 2x2x4 slice. The times are simulated.
32 devices in a mesh: vox: 16 (over z, y, core), star: 2 (over x).
Axes of the slice: x: 2, y: 2, z: 4, core: 2. Of those that a mesh axis runs over, the one named last changes fastest.
Arguments:
- mean_field: float32 [32, 128, 128], P('vox', 'star'), may hold values from -3 to 3
- deviations: float32 [4, 32, 128, 128], P(None, 'vox', 'star'), may hold values from -4 to 4
- stencil: float32 [3, 3], replicated, may hold values from -2 to 2
- vertical_mix: float32 [128, 128], replicated, may hold values from -0.5 to 0.5
- log_mean: float32 [128], replicated, may hold values from -1.6 to -0.4
- responses: bfloat16 [3072, 128, 128], P(('vox', 'star')), may hold values from 0 to 0.015625
- pair_line: int32 [3072], P(('vox', 'star')), may hold values from 0 to 127
- pair_owner: int32 [3072, 1], P(('vox', 'star')), may hold values from 0 to 15; in each aligned block of 96 rows (0 to 95, 96 to 191, ...) at most 12 rows name the same one
- pair_star: int32 [3072], P(('vox', 'star')), may hold values from 0 to 7
- observed: float32 [256, 128], P(('vox', 'star')), may hold values from 0 to 15
- inv_var: float32 [256, 128], P(('vox', 'star')), may hold values from 0.05 to 0.5
Outputs:
- gradient: float32 [32, 128, 128], P('vox', 'star')
- residual_mean: float32 [256, 128], P(('vox', 'star'))
Inputs may be any that keep to these rules, and one draw needn't show every extreme that they name: `pair_owner`: among the 96 pairs of one device at most 12 name one owner, a bound that some block reaches.
All inputs are finite; a program needn't handle non-finite values.
Results may differ from a plain program's by a relative error of at most 0.0015.
Values may be sent and summed in bfloat16 or wider, within the bound.
No kernel may reach another device: no remote copies, remote signals or barrier semaphores. Data moves between devices by JAX's collectives and lax.ppermute only.
A program may use at most 64 MiB of HBM per device.

v0:
```python
import jax
import jax.numpy as jnp
from jax import lax
from jax.sharding import PartitionSpec as P

HIGH = lax.Precision.HIGHEST


def with_halo(cells, sides, width):
    for axis, dim in sides:
        count = lax.axis_size(axis)
        ends = count - 1
        head = lax.slice_in_dim(cells, 0, width, axis=dim)
        tail = lax.slice_in_dim(cells, cells.shape[dim] - width, cells.shape[dim], axis=dim)
        cells = jnp.concatenate(
            [
                lax.ppermute(tail, axis, [(i, (i + 1) % count) for i in range(ends)]),
                cells,
                lax.ppermute(head, axis, [((i + 1) % count, i) for i in range(ends)]),
            ],
            axis=dim,
        )
    return cells


def per_device(
    mean_field,
    deviations,
    stencil,
    vertical_mix,
    log_mean,
    responses,
    pair_line,
    pair_owner,
    pair_star,
    observed,
    inv_var,
):
    samples = deviations.shape[0]
    width_x = deviations.shape[1]
    width_y = deviations.shape[2]
    length = deviations.shape[3]
    pair_count = responses.shape[0]
    block_count = observed.shape[0]
    group_size = lax.axis_size("vox")
    latent = mean_field[None] + deviations
    padded = with_halo(latent, (("vox", 1), ("star", 2)), 1)
    smoothed = jnp.zeros(latent.shape, jnp.float32)
    for offset_x in range(3):
        for offset_y in range(3):
            smoothed = (
                smoothed
                + stencil[offset_x, offset_y]
                * padded[:, offset_x : offset_x + width_x, offset_y : offset_y + width_y, :]
            )
    log_density = jnp.einsum("sxyw,zw->sxyz", smoothed, vertical_mix, precision=HIGH) + log_mean
    density = jnp.exp(log_density)
    density_b = density.astype(jnp.bfloat16).reshape(samples, width_x * width_y, length)
    picked = jnp.take(density_b, pair_line, axis=1)
    contribution = jnp.einsum("pij,spj->psi", responses, picked, preferred_element_type=jnp.float32)
    star_count = observed.shape[0]
    group_blocks = group_size * star_count
    target = pair_owner[:, 0] * star_count + pair_star
    target_onehot = (target[:, None] == jnp.arange(group_blocks, dtype=jnp.int32)[None, :]).astype(
        jnp.float32
    )
    partial = jnp.einsum("pb,psi->bsi", target_onehot, contribution, precision=HIGH)
    extinction = lax.psum(partial, "vox")
    table = lax.all_gather(jnp.stack([observed, inv_var]), "vox", axis=1, tiled=True)
    misfit = table[1][:, None, :] * (extinction - table[0][:, None, :])
    misfit_b = misfit.astype(jnp.bfloat16)
    own = lax.dynamic_slice_in_dim(misfit, lax.axis_index("vox") * star_count, star_count, axis=0)
    residual_mean = jnp.mean(own, axis=1)
    pair_misfit = jnp.take(misfit_b, target, axis=0)
    pair_adjoint = jnp.einsum(
        "pij,psi->psj", responses, pair_misfit, preferred_element_type=jnp.float32
    )
    line_onehot = (
        pair_line[:, None] == jnp.arange(width_x * width_y, dtype=jnp.int32)[None, :]
    ).astype(jnp.float32)
    adjoint = jnp.einsum("pb,psj->sbj", line_onehot, pair_adjoint, precision=HIGH).reshape(
        samples, width_x, width_y, length
    )
    grad_log = density * adjoint
    grad_smooth = jnp.einsum("sxyz,zw->sxyw", grad_log, vertical_mix, precision=HIGH)
    padded_grad = with_halo(grad_smooth, (("vox", 1), ("star", 2)), 1)
    grad_latent = jnp.zeros(latent.shape, jnp.float32)
    for offset_x in range(3):
        for offset_y in range(3):
            grad_latent = (
                grad_latent
                + stencil[offset_x, offset_y]
                * padded_grad[
                    :,
                    2 - offset_x : 2 - offset_x + width_x,
                    2 - offset_y : 2 - offset_y + width_y,
                    :,
                ]
            )
    gradient = jnp.mean(grad_latent + latent, axis=0)
    return (gradient, residual_mean)


def solution(mesh):
    placed = (
        P("vox", "star", None),
        P(None, "vox", "star", None),
        P(),
        P(),
        P(),
        P(("vox", "star"), None, None),
        P(("vox", "star")),
        P(("vox", "star"), None),
        P(("vox", "star")),
        P(("vox", "star"), None),
        P(("vox", "star"), None),
    )
    return jax.shard_map(
        per_device,
        mesh=mesh,
        in_specs=placed,
        out_specs=(P("vox", "star", None), P(("vox", "star"), None)),
        check_vma=False,
    )
```

profile of v0, /device:TPU:7, one launch (start us, length us, event | category | flops | bytes accessed | tf_op | source)
XLA Modules:
  0.0 185.1 jit_solution(6022717707829478496)
XLA Ops:
  7.2 1.1 broadcast_add_fusion
  8.4 3.7 %collective-permute-start = (f32[4,1,64,128]{3,2,1,0:T(8,128)S(1)}, f32[4,1,64,128]{3,2,1,0:T(8,128)S(1)}, u32[]{:S(2)}, u32[]{:S(2)}) collective-permute-start(f32[4,1,64,128]{3,2,1,0:T(8,128)S(1)} %get-tuple-element.16), channel_id=1, source_target_pairs={{0,2},{2,4},{4,6},{6,8},{8,10},{10,12},{12,14},{14,16},{16,18},{18... | collective-permute-start | bytes 393224 | tf_op jit(solution)/shard_map/ppermute | solution.py:17
  12.1 1.9 %collective-permute-start.1 = (f32[4,1,64,128]{3,2,1,0:T(8,128)S(1)}, f32[4,1,64,128]{3,2,1,0:T(8,128)S(1)}, u32[]{:S(2)}, u32[]{:S(2)}) collective-permute-start(f32[4,1,64,128]{3,2,1,0:T(8,128)S(1)} %get-tuple-element.17), channel_id=1, source_target_pairs={{2,0},{4,2},{6,4},{8,6},{10,8},{12,10},{14,12},{16,14},{18,16},{20... | collective-permute-start | bytes 393224 | tf_op jit(solution)/shard_map/ppermute | solution.py:19
  15.4 19.6 %all_gather.3 = f32[2,128,128]{2,1,0:T(8,128)S(1)} all-gather(f32[2,8,128]{2,1,0:T(8,128)S(1)} %pad_maximum_fusion.12), channel_id=1, replica_groups=mesh['vox'=16,'star'=2] {'vox'}, dimensions={1}, use_global_device_ids=true | all-gather | bytes 139264 | tf_op jit(solution)/shard_map/all_gather | solution.py:69
  36.4 1.7 fusion.71
  38.1 1.3 collective-permute-start.2
  39.4 4.0 %collective-permute-start.3 = (f32[4,4,1,128]{3,2,1,0:T(1,128)S(1)}, f32[4,4,1,128]{3,2,1,0:T(1,128)S(1)}, u32[]{:S(2)}, u32[]{:S(2)}) collective-permute-start(f32[4,4,1,128]{3,2,1,0:T(1,128)S(1)} %get-tuple-element.13), channel_id=1, source_target_pairs={{1,0},{3,2},{5,4},{7,6},{9,8},{11,10},{13,12},{15,14},{17,16},{19,... | collective-permute-start | bytes 24584 | tf_op jit(solution)/shard_map/ppermute | solution.py:19
  43.4 0.8 collective-permute-done.3
  44.3 6.8 %fusion.72 = (bf16[4,2,64,128]{3,2,1,0:T(8,128)(2,1)S(1)}, f32[4,2,64,128]{3,2,1,0:T(8,128)}) fusion(f32[128]{0:T(128)S(1)} %copy-done.5, f32[128,128]{1,0:T(8,128)S(1)} %copy-done.2, f32[4,4,65,128]{3,2,1,0:T(8,128)S(1)} %get-tuple-element.11, f32[4,1,64,128]{3,2,1,0:T(8,128)S(1)} %collective-permute-done.1, f32[4,2,64,128]{3,2,1,0:T(8,128)S(1)} %broadcast_add_fusion, ...), kind=kOutput, calls=%fused_computation.109 | convolution fusion | flops 102039552 | bytes 2556452 | tf_op jit(solution)/shard_map/sxyw,zw->sxyz/dot_general | solution.py:56
  51.9 1.8 fusion.48
  53.7 1.1 fusion.37
  54.8 89.7 %all-reduce.2.cloned.1.call-done = f32[128,4,128]{2,0,1:T(8,128)} async-done(((f32[128,4,128]{2,0,1:T(8,128)}), f32[128,4,128]{2,0,1:T(8,128)}) %all-reduce.2.cloned.1.call-update) | async-done | bytes 262160 | tf_op jit(solution)/shard_map/psum | solution.py:68
  144.5 1.7 fusion.68
  147.0 1.0 fusion.51
  148.8 0.7 fusion.69
  149.6 5.3 %collective-permute-start.4 = (f32[4,1,64,128]{3,2,1,0:T(8,128)}, f32[4,1,64,128]{3,2,1,0:T(8,128)S(1)}, u32[]{:S(2)}, u32[]{:S(2)}) collective-permute-start(f32[4,1,64,128]{3,2,1,0:T(8,128)} %get-tuple-element.14), channel_id=1, source_target_pairs={{0,2},{2,4},{4,6},{6,8},{8,10},{10,12},{12,14},{14,16},{16,18},{18... | collective-permute-start | bytes 393224 | tf_op jit(solution)/shard_map/ppermute | solution.py:17
  154.8 1.9 %collective-permute-start.5 = (f32[4,1,64,128]{3,2,1,0:T(8,128)}, f32[4,1,64,128]{3,2,1,0:T(8,128)}, u32[]{:S(2)}, u32[]{:S(2)}) collective-permute-start(f32[4,1,64,128]{3,2,1,0:T(8,128)} %get-tuple-element.15), channel_id=1, source_target_pairs={{2,0},{4,2},{6,4},{8,6},{10,8},{12,10},{14,12},{16,14},{18,16},{20... | collective-permute-start | bytes 393224 | tf_op jit(solution)/shard_map/ppermute | solution.py:19
  157.5 4.8 %collective-permute-done.5 = f32[4,1,64,128]{3,2,1,0:T(8,128)} collective-permute-done((f32[4,1,64,128]{3,2,1,0:T(8,128)}, f32[4,1,64,128]{3,2,1,0:T(8,128)}, u32[]{:S(2)}, u32[]{:S(2)}) %collective-permute-start.5) | collective-permute-done | bytes 131104 | tf_op jit(solution)/shard_map/ppermute | solution.py:19
  162.3 0.7 pad_maximum_fusion.8
  163.1 2.2 %collective-permute-start.6 = (f32[4,4,1,128]{3,2,1,0:T(1,128)S(1)}, f32[4,4,1,128]{3,2,1,0:T(1,128)S(1)}, u32[]{:S(2)}, u32[]{:S(2)}) collective-permute-start(f32[4,4,1,128]{3,2,1,0:T(1,128)S(1)} %get-tuple-element.8), channel_id=1, source_target_pairs={{1,0},{3,2},{5,4},{7,6},{9,8},{11,10},{13,12},{15,14},{17,16},{19,... | collective-permute-start | bytes 24584 | tf_op jit(solution)/shard_map/ppermute | solution.py:19
  165.3 1.3 collective-permute-start.7
  167.2 2.5 %collective-permute-done.7 = f32[4,4,1,128]{3,2,1,0:T(1,128)S(1)} collective-permute-done((f32[4,4,1,128]{3,2,1,0:T(1,128)S(1)}, f32[4,4,1,128]{3,2,1,0:T(1,128)S(1)}, u32[]{:S(2)}, u32[]{:S(2)}) %collective-permute-start.7) | collective-permute-done | bytes 8224 | tf_op jit(solution)/shard_map/ppermute | solution.py:17
  169.7 1.1 pad_maximum_fusion.1
  170.7 6.9 %fusion.3 = f32[2,64,128]{2,1,0:T(8,128)S(1)} fusion(f32[4,4,65,128]{3,2,1,0:T(8,128)S(1)} %get-tuple-element.7, f32[4,2,64,128]{3,2,1,0:T(8,128)S(1)} %fusion.32, f32[4,1,64,128]{3,2,1,0:T(8,128)S(1)} %collective-permute-done.4, f32[4,4,65,128]{3,2,1,0:T(8,128)S(1)} %get-tuple-element.6, f32[4,1,64,128]{3,2,1,0:T(8,128)} %collective-permute-done.5, ...), kind=kLoop, calls=%fused_computation.11 | loop fusion | flops 1425408 | bytes 2490404 | tf_op jit(solution)/shard_map/reduce_sum | solution.py:100
  (39 shorter events, 7.3 us)
Async XLA Ops:
  7.2 44.8 %copy-start = (bf16[96,128,128]{2,1,0:T(8,128)(2,1)S(1)}, bf16[96,128,128]{2,1,0:T(8,128)(2,1)}, u32[]{:S(2)}) copy-start(bf16[96,128,128]{2,1,0:T(8,128)(2,1)} %param.16) | copy-start | bytes 9437188
  7.2 37.1 %copy-start.2 = (f32[128,128]{1,0:T(8,128)S(1)}, f32[128,128]{1,0:T(8,128)}, u32[]{:S(2)}) copy-start(f32[128,128]{1,0:T(8,128)} %param.14) | copy-start | bytes 196612
  7.2 37.1 %copy-start.5 = (f32[128]{0:T(128)S(1)}, f32[128]{0:T(128)}, u32[]{:S(2)}) copy-start(f32[128]{0:T(128)} %param.15) | copy-start | bytes 1540
  7.2 137.3 %all-reduce.2.cloned.1.call-start = ((), (), s32[]{:S(2)}) async-start(), calls=%async_computation | async-start | bytes 524288 | tf_op jit(solution)/shard_map/psum | solution.py:68
  8.4 29.7 %collective-permute-start = (f32[4,1,64,128]{3,2,1,0:T(8,128)S(1)}, f32[4,1,64,128]{3,2,1,0:T(8,128)S(1)}, u32[]{:S(2)}, u32[]{:S(2)}) collective-permute-start(f32[4,1,64,128]{3,2,1,0:T(8,128)S(1)} %get-tuple-element.16), channel_id=1, source_target_pairs={{0,2},{2,4},{4,6},{6,8},{8,10},{10,12},{12,14},{14,16},{16,18},{18... | collective-permute-start | bytes 393224 | tf_op jit(solution)/shard_map/ppermute | solution.py:17
  12.1 26.0 %collective-permute-start.1 = (f32[4,1,64,128]{3,2,1,0:T(8,128)S(1)}, f32[4,1,64,128]{3,2,1,0:T(8,128)S(1)}, u32[]{:S(2)}, u32[]{:S(2)}) collective-permute-start(f32[4,1,64,128]{3,2,1,0:T(8,128)S(1)} %get-tuple-element.17), channel_id=1, source_target_pairs={{2,0},{4,2},{6,4},{8,6},{10,8},{12,10},{14,12},{16,14},{18,16},{20... | collective-permute-start | bytes 393224 | tf_op jit(solution)/shard_map/ppermute | solution.py:19
  38.1 5.3 %collective-permute-start.2 = (f32[4,4,1,128]{3,2,1,0:T(1,128)S(1)}, f32[4,4,1,128]{3,2,1,0:T(1,128)S(1)}, u32[]{:S(2)}, u32[]{:S(2)}) collective-permute-start(f32[4,4,1,128]{3,2,1,0:T(1,128)S(1)} %get-tuple-element.12), channel_id=1, source_target_pairs={{0,1},{2,3},{4,5},{6,7},{8,9},{10,11},{12,13},{14,15},{16,17},{18,... | collective-permute-start | bytes 24584 | tf_op jit(solution)/shard_map/ppermute | solution.py:17
  39.4 4.8 %collective-permute-start.3 = (f32[4,4,1,128]{3,2,1,0:T(1,128)S(1)}, f32[4,4,1,128]{3,2,1,0:T(1,128)S(1)}, u32[]{:S(2)}, u32[]{:S(2)}) collective-permute-start(f32[4,4,1,128]{3,2,1,0:T(1,128)S(1)} %get-tuple-element.13), channel_id=1, source_target_pairs={{1,0},{3,2},{5,4},{7,6},{9,8},{11,10},{13,12},{15,14},{17,16},{19,... | collective-permute-start | bytes 24584 | tf_op jit(solution)/shard_map/ppermute | solution.py:19
  53.7 94.3 %copy-start.4 = (s32[96]{0:T(128)S(1)}, s32[96]{0:T(128)}, u32[]{:S(2)}) copy-start(s32[96]{0:T(128)} %param.17) | copy-start | bytes 1156
  53.7 94.7 %copy-start.3 = (f32[128,128]{1,0:T(8,128)S(1)}, f32[128,128]{1,0:T(8,128)}, u32[]{:S(2)}) copy-start(f32[128,128]{1,0:T(8,128)} %param.14) | copy-start | bytes 196612
  147.0 1.4 copy-start.1
  149.6 7.9 %collective-permute-start.4 = (f32[4,1,64,128]{3,2,1,0:T(8,128)}, f32[4,1,64,128]{3,2,1,0:T(8,128)S(1)}, u32[]{:S(2)}, u32[]{:S(2)}) collective-permute-start(f32[4,1,64,128]{3,2,1,0:T(8,128)} %get-tuple-element.14), channel_id=1, source_target_pairs={{0,2},{2,4},{4,6},{6,8},{8,10},{10,12},{12,14},{14,16},{16,18},{18... | collective-permute-start | bytes 393224 | tf_op jit(solution)/shard_map/ppermute | solution.py:17
  154.8 7.5 %collective-permute-start.5 = (f32[4,1,64,128]{3,2,1,0:T(8,128)}, f32[4,1,64,128]{3,2,1,0:T(8,128)}, u32[]{:S(2)}, u32[]{:S(2)}) collective-permute-start(f32[4,1,64,128]{3,2,1,0:T(8,128)} %get-tuple-element.15), channel_id=1, source_target_pairs={{2,0},{4,2},{6,4},{8,6},{10,8},{12,10},{14,12},{16,14},{18,16},{20... | collective-permute-start | bytes 393224 | tf_op jit(solution)/shard_map/ppermute | solution.py:19
  163.1 4.1 %collective-permute-start.6 = (f32[4,4,1,128]{3,2,1,0:T(1,128)S(1)}, f32[4,4,1,128]{3,2,1,0:T(1,128)S(1)}, u32[]{:S(2)}, u32[]{:S(2)}) collective-permute-start(f32[4,4,1,128]{3,2,1,0:T(1,128)S(1)} %get-tuple-element.8), channel_id=1, source_target_pairs={{1,0},{3,2},{5,4},{7,6},{9,8},{11,10},{13,12},{15,14},{17,16},{19,... | collective-permute-start | bytes 24584 | tf_op jit(solution)/shard_map/ppermute | solution.py:19
  165.3 4.4 %collective-permute-start.7 = (f32[4,4,1,128]{3,2,1,0:T(1,128)S(1)}, f32[4,4,1,128]{3,2,1,0:T(1,128)S(1)}, u32[]{:S(2)}, u32[]{:S(2)}) collective-permute-start(f32[4,4,1,128]{3,2,1,0:T(1,128)S(1)} %get-tuple-element.9), channel_id=1, source_target_pairs={{0,1},{2,3},{4,5},{6,7},{8,9},{10,11},{12,13},{14,15},{16,17},{18,... | collective-permute-start | bytes 24584 | tf_op jit(solution)/shard_map/ppermute | solution.py:17
Sparse Core Ops, SparseCore 0:
  54.9 89.5 all-reduce.1
where the time goes:
time: 186 us; the launch traced here: 185 us
  waiting for transfers between devices  97.8 us (53%)
  starting transfers between devices  21.6 us (12%)
  blocking collectives  19.6 us (11%)
  other arithmetic  16.3 us (9%)
  between operations  14.3 us (8%)
  matrix products  11.4 us (6%)
  local copies, waits for them, and re-layouts  4.09 us (2%)
    psum x1, waiting for transfers between devices, per_device(): extinction = lax.psum(partial, 'vox')  89.7 us
    all_gather x1, blocking collectives, per_device(): lax.all_gather(jnp.stack([observed, inv_var]), 'vox', axis=1, tiled=True)  19.6 us
    ppermute x4, starting transfers between devices, with_halo(): lax.ppermute(tail, axis, [(i, (i + 1) % count) for i in range(ends)])  11.6 us
    ppermute x4, starting transfers between devices, with_halo(): lax.ppermute(head, axis, [((i + 1) % count, i) for i in range(ends)])  10 us
    reduce_sum x1, other arithmetic, per_device(): gradient = jnp.mean(grad_latent + latent, axis=0)  6.87 us
    dot_general x1, matrix products, per_device(): jnp.einsum('sxyw,zw->sxyz', smoothed, vertical_mix, precision=HIGH)  6.84 us
    ppermute x4, waiting for transfers between devices, with_halo(): lax.ppermute(head, axis, [((i + 1) % count, i) for i in range(ends)])  5.59 us
  transfers between devices with their start and end apart: 9, of which 4 were waited for; matrix products, arithmetic and copies ran while one was open for 3% of the time, Pallas kernels for 0%

commit v1 on v0

--- a/solution.py
+++ b/solution.py
@@ -66,7 +66,17 @@
     )
     partial = jnp.einsum("pb,psi->bsi", target_onehot, contribution, precision=HIGH)
     extinction = lax.psum(partial, "vox")
-    table = lax.all_gather(jnp.stack([observed, inv_var]), "vox", axis=1, tiled=True)
+    x = jnp.stack([observed, inv_var])
+    ways = lax.axis_size("vox")
+    up = [(d, (d + 1) % ways) for d in range(ways)]
+    down = [(d, (d - 1) % ways) for d in range(ways)]
+    earlier, later = ([x], [x])
+    for _ in range(ways // 2):
+        earlier.append(lax.ppermute(earlier[-1], "vox", up))
+    for _ in range((ways - 1) // 2):
+        later.append(lax.ppermute(later[-1], "vox", down))
+    line = jnp.concatenate([*earlier[::-1], *later[1:]], axis=1)
+    table = jnp.roll(line, (lax.axis_index("vox") - ways // 2) * x.shape[1], axis=1)
     misfit = table[1][:, None, :] * (extinction - table[0][:, None, :])
     misfit_b = misfit.astype(jnp.bfloat16)
     own = lax.dynamic_slice_in_dim(misfit, lax.axis_index("vox") * star_count, star_count, axis=0)

time: 186 us -> 224 us (1.20)
  the two profiles are of different devices: /device:TPU:7 before, /device:TPU:10 now
where the time goes in v1:
time: 224 us; the launch traced here: 222 us
  waiting for transfers between devices  110 us (49%)
  starting transfers between devices  39.3 us (18%)
  local copies, waits for them, and re-layouts  24 us (11%)
  other arithmetic  20.6 us (9%)
  between operations  14.3 us (6%)
  matrix products  13.9 us (6%)
    psum x1, waiting for transfers between devices, per_device(): extinction = lax.psum(partial, 'vox')  96.1 us
    ppermute x7, starting transfers between devices, per_device(): later.append(lax.ppermute(later[-1], 'vox', down))  18.7 us
    unnamed x63, local copies, waits for them, and re-layouts  17.5 us
    ppermute x4, starting transfers between devices, with_halo(): lax.ppermute(head, axis, [((i + 1) % count, i) for i in range(ends)])  13.4 us
    ppermute x4, waiting for transfers between devices, with_halo(): lax.ppermute(tail, axis, [(i, (i + 1) % count) for i in range(ends)])  8 us
    dot_general x1, matrix products, per_device(): jnp.einsum('sxyw,zw->sxyz', smoothed, vertical_mix, precision=HIGH)  7.82 us
    reduce_sum x1, other arithmetic, per_device(): gradient = jnp.mean(grad_latent + latent, axis=0)  6.92 us
    ppermute x4, starting transfers between devices, with_halo(): lax.ppermute(tail, axis, [(i, (i + 1) % count) for i in range(ends)])  6.91 us
  transfers between devices with their start and end apart: 24, of which 11 were waited for; matrix products, arithmetic and copies ran while one was open for 12% of the time, Pallas kernels for 0%

profile of v1, /device:TPU:10, one launch (start us, length us, event | category | flops | bytes accessed | tf_op | source)
XLA Modules:
  0.0 221.8 jit_solution(11956006830069172367)
XLA Ops:
  8.1 2.6 %collective-permute-start.12 = (f32[2,8,128]{2,1,0:T(8,128)S(1)}, f32[2,8,128]{2,1,0:T(8,128)S(1)}, u32[]{:S(2)}, u32[]{:S(2)}) collective-permute-start(f32[2,8,128]{2,1,0:T(8,128)S(1)} %pad_maximum_fusion.12), channel_id=1, source_target_pairs={{0,30},{2,0},{4,2},{6,4},{8,6},{10,8},{12,10},{14,12},{16,14},{18,... | collective-permute-start | bytes 24584 | tf_op jit(solution)/shard_map/ppermute | solution.py:77
  12.8 4.5 %collective-permute-start.1 = (f32[4,1,64,128]{3,2,1,0:T(8,128)}, f32[4,1,64,128]{3,2,1,0:T(8,128)S(1)}, u32[]{:S(2)}, u32[]{:S(2)}) collective-permute-start(f32[4,1,64,128]{3,2,1,0:T(8,128)} %get-tuple-element.19), channel_id=1, source_target_pairs={{2,0},{4,2},{6,4},{8,6},{10,8},{12,10},{14,12},{16,14},{18,16},{20... | collective-permute-start | bytes 393224 | tf_op jit(solution)/shard_map/ppermute | solution.py:19
  17.3 1.9 collective-permute-start
  20.6 2.7 %collective-permute-start.13 = (f32[2,8,128]{2,1,0:T(8,128)S(1)}, f32[2,8,128]{2,1,0:T(8,128)S(1)}, u32[]{:S(2)}, u32[]{:S(2)}) collective-permute-start(f32[2,8,128]{2,1,0:T(8,128)S(1)} %collective-permute-done.12), channel_id=1, source_target_pairs={{0,30},{2,0},{4,2},{6,4},{8,6},{10,8},{12,10},{14,12},{16,14},{18,... | collective-permute-start | bytes 24584 | tf_op jit(solution)/shard_map/ppermute | solution.py:77
  23.3 1.5 collective-permute-done.6
  25.5 2.7 %collective-permute-start.14 = (f32[2,8,128]{2,1,0:T(8,128)S(1)}, f32[2,8,128]{2,1,0:T(8,128)S(1)}, u32[]{:S(2)}, u32[]{:S(2)}) collective-permute-start(f32[2,8,128]{2,1,0:T(8,128)S(1)} %collective-permute-done.13), channel_id=1, source_target_pairs={{0,30},{2,0},{4,2},{6,4},{8,6},{10,8},{12,10},{14,12},{16,14},{18,... | collective-permute-start | bytes 24584 | tf_op jit(solution)/shard_map/ppermute | solution.py:77
  29.6 2.6 %collective-permute-start.15 = (f32[2,8,128]{2,1,0:T(8,128)S(1)}, f32[2,8,128]{2,1,0:T(8,128)S(1)}, u32[]{:S(2)}, u32[]{:S(2)}) collective-permute-start(f32[2,8,128]{2,1,0:T(8,128)S(1)} %collective-permute-done.14), channel_id=1, source_target_pairs={{0,30},{2,0},{4,2},{6,4},{8,6},{10,8},{12,10},{14,12},{16,14},{18,... | collective-permute-start | bytes 24584 | tf_op jit(solution)/shard_map/ppermute | solution.py:77
  32.8 1.7 fusion.71
  34.5 2.7 %collective-permute-start.16 = (f32[2,8,128]{2,1,0:T(8,128)S(1)}, f32[2,8,128]{2,1,0:T(8,128)}, u32[]{:S(2)}, u32[]{:S(2)}) collective-permute-start(f32[2,8,128]{2,1,0:T(8,128)S(1)} %collective-permute-done.15), channel_id=1, source_target_pairs={{0,30},{2,0},{4,2},{6,4},{8,6},{10,8},{12,10},{14,12},{16,14},{18,... | collective-permute-start | bytes 24584 | tf_op jit(solution)/shard_map/ppermute | solution.py:77
  38.6 2.7 %collective-permute-start.17 = (f32[2,8,128]{2,1,0:T(8,128)}, f32[2,8,128]{2,1,0:T(8,128)}, u32[]{:S(2)}, u32[]{:S(2)}) collective-permute-start(f32[2,8,128]{2,1,0:T(8,128)} %collective-permute-done.16), channel_id=1, source_target_pairs={{0,30},{2,0},{4,2},{6,4},{8,6},{10,8},{12,10},{14,12},{16,14},{18,... | collective-permute-start | bytes 24584 | tf_op jit(solution)/shard_map/ppermute | solution.py:77
  42.9 2.7 %collective-permute-start.18 = (f32[2,8,128]{2,1,0:T(8,128)}, f32[2,8,128]{2,1,0:T(8,128)S(1)}, u32[]{:S(2)}, u32[]{:S(2)}) collective-permute-start(f32[2,8,128]{2,1,0:T(8,128)} %collective-permute-done.17), channel_id=1, source_target_pairs={{0,30},{2,0},{4,2},{6,4},{8,6},{10,8},{12,10},{14,12},{16,14},{18,... | collective-permute-start | bytes 24584 | tf_op jit(solution)/shard_map/ppermute | solution.py:77
  65.2 4.5 %collective-permute-start.3 = (f32[4,4,1,128]{3,2,1,0:T(1,128)S(1)}, f32[4,4,1,128]{3,2,1,0:T(1,128)S(1)}, u32[]{:S(2)}, u32[]{:S(2)}) collective-permute-start(f32[4,4,1,128]{3,2,1,0:T(1,128)S(1)} %get-tuple-element.13), channel_id=1, source_target_pairs={{1,0},{3,2},{5,4},{7,6},{9,8},{11,10},{13,12},{15,14},{17,16},{19,... | collective-permute-start | bytes 24584 | tf_op jit(solution)/shard_map/ppermute | solution.py:19
  72.2 7.8 %fusion.72 = (bf16[4,2,64,128]{3,2,1,0:T(8,128)(2,1)S(1)}, f32[4,2,64,128]{3,2,1,0:T(8,128)}) fusion(f32[128]{0:T(128)} %param.15, f32[128,128]{1,0:T(8,128)} %param.14, f32[4,4,65,128]{3,2,1,0:T(8,128)S(1)} %get-tuple-element.11, f32[4,1,64,128]{3,2,1,0:T(8,128)S(1)} %collective-permute-done.1, f32[4,2,64,128]{3,2,1,0:T(8,128)S(1)} %broadcast_add_fusion, ...), kind=kOutput, calls=%fused_computation.141 | convolution fusion | flops 102039552 | bytes 2556452 | tf_op jit(solution)/shard_map/sxyw,zw->sxyz/dot_general | solution.py:56
  81.0 1.8 fusion.48
  82.8 1.8 fusion.37
  86.1 96.1 %all-reduce.2.cloned.1.call-done = f32[128,4,128]{2,0,1:T(8,128)} async-done(((f32[128,4,128]{2,0,1:T(8,128)}), f32[128,4,128]{2,0,1:T(8,128)}) %all-reduce.2.cloned.1.call-update) | async-done | bytes 262160 | tf_op jit(solution)/shard_map/psum | solution.py:68
  182.1 1.7 fusion.68
  188.1 1.9 collective-permute-start.20
  190.0 2.4 %collective-permute-start.19 = (f32[4,1,64,128]{3,2,1,0:T(8,128)}, f32[4,1,64,128]{3,2,1,0:T(8,128)}, u32[]{:S(2)}, u32[]{:S(2)}) collective-permute-start(f32[4,1,64,128]{3,2,1,0:T(8,128)} %get-tuple-element.14), channel_id=1, source_target_pairs={{0,2},{2,4},{4,6},{6,8},{8,10},{10,12},{12,14},{14,16},{16,18},{18... | collective-permute-start | bytes 393224 | tf_op jit(solution)/shard_map/ppermute | solution.py:17
  193.2 4.4 %collective-permute-done.19 = f32[4,1,64,128]{3,2,1,0:T(8,128)} collective-permute-done((f32[4,1,64,128]{3,2,1,0:T(8,128)}, f32[4,1,64,128]{3,2,1,0:T(8,128)}, u32[]{:S(2)}, u32[]{:S(2)}) %collective-permute-start.19) | collective-permute-done | bytes 131104 | tf_op jit(solution)/shard_map/ppermute | solution.py:17
  198.3 2.5 %collective-permute-start.21 = (f32[4,4,1,128]{3,2,1,0:T(1,128)S(1)}, f32[4,4,1,128]{3,2,1,0:T(1,128)S(1)}, u32[]{:S(2)}, u32[]{:S(2)}) collective-permute-start(f32[4,4,1,128]{3,2,1,0:T(1,128)S(1)} %get-tuple-element.8), channel_id=1, source_target_pairs={{1,0},{3,2},{5,4},{7,6},{9,8},{11,10},{13,12},{15,14},{17,16},{19,... | collective-permute-start | bytes 24584 | tf_op jit(solution)/shard_map/ppermute | solution.py:19
  200.7 1.3 collective-permute-start.22
  202.6 3.6 %collective-permute-done.22 = f32[4,4,1,128]{3,2,1,0:T(1,128)S(1)} collective-permute-done((f32[4,4,1,128]{3,2,1,0:T(1,128)S(1)}, f32[4,4,1,128]{3,2,1,0:T(1,128)S(1)}, u32[]{:S(2)}, u32[]{:S(2)}) %collective-permute-start.22) | collective-permute-done | bytes 8224 | tf_op jit(solution)/shard_map/ppermute | solution.py:17
  207.4 6.9 %fusion.3 = f32[2,64,128]{2,1,0:T(8,128)S(1)} fusion(f32[4,4,65,128]{3,2,1,0:T(8,128)S(1)} %get-tuple-element.7, f32[4,2,64,128]{3,2,1,0:T(8,128)S(1)} %fusion.32, f32[4,1,64,128]{3,2,1,0:T(8,128)} %collective-permute-done.19, f32[4,4,65,128]{3,2,1,0:T(8,128)S(1)} %get-tuple-element.6, f32[4,1,64,128]{3,2,1,0:T(8,128)S(1)} %collective-permute-done.20, ...), kind=kLoop, calls=%fused_computation.11 | loop fusion | flops 1425408 | bytes 2490404 | tf_op jit(solution)/shard_map/reduce_sum | solution.py:110
  (121 shorter events, 42.4 us)
Async XLA Ops:
  7.2 175.0 %all-reduce.2.cloned.1.call-start = ((), (), s32[]{:S(2)}) async-start(), calls=%async_computation | async-start | bytes 524288 | tf_op jit(solution)/shard_map/psum | solution.py:68
  8.1 4.0 %collective-permute-start.4 = (f32[2,8,128]{2,1,0:T(8,128)S(1)}, f32[2,8,128]{2,1,0:T(8,128)S(1)}, u32[]{:S(2)}, u32[]{:S(2)}) collective-permute-start(f32[2,8,128]{2,1,0:T(8,128)S(1)} %pad_maximum_fusion.12), channel_id=1, source_target_pairs={{0,2},{2,4},{4,6},{6,8},{8,10},{10,12},{12,14},{14,16},{16,18},{18... | collective-permute-start | bytes 24584 | tf_op jit(solution)/shard_map/ppermute | solution.py:75
  8.1 12.5 %collective-permute-start.12 = (f32[2,8,128]{2,1,0:T(8,128)S(1)}, f32[2,8,128]{2,1,0:T(8,128)S(1)}, u32[]{:S(2)}, u32[]{:S(2)}) collective-permute-start(f32[2,8,128]{2,1,0:T(8,128)S(1)} %pad_maximum_fusion.12), channel_id=1, source_target_pairs={{0,30},{2,0},{4,2},{6,4},{8,6},{10,8},{12,10},{14,12},{16,14},{18,... | collective-permute-start | bytes 24584 | tf_op jit(solution)/shard_map/ppermute | solution.py:77
  12.1 7.2 %collective-permute-start.5 = (f32[2,8,128]{2,1,0:T(8,128)S(1)}, f32[2,8,128]{2,1,0:T(8,128)S(1)}, u32[]{:S(2)}, u32[]{:S(2)}) collective-permute-start(f32[2,8,128]{2,1,0:T(8,128)S(1)} %collective-permute-done.4), channel_id=1, source_target_pairs={{0,2},{2,4},{4,6},{6,8},{8,10},{10,12},{12,14},{14,16},{16,18},{18... | collective-permute-start | bytes 24584 | tf_op jit(solution)/shard_map/ppermute | solution.py:75
  12.8 50.3 %collective-permute-start.1 = (f32[4,1,64,128]{3,2,1,0:T(8,128)}, f32[4,1,64,128]{3,2,1,0:T(8,128)S(1)}, u32[]{:S(2)}, u32[]{:S(2)}) collective-permute-start(f32[4,1,64,128]{3,2,1,0:T(8,128)} %get-tuple-element.19), channel_id=1, source_target_pairs={{2,0},{4,2},{6,4},{8,6},{10,8},{12,10},{14,12},{16,14},{18,16},{20... | collective-permute-start | bytes 393224 | tf_op jit(solution)/shard_map/ppermute | solution.py:19
  17.3 45.8 %collective-permute-start = (f32[4,1,64,128]{3,2,1,0:T(8,128)}, f32[4,1,64,128]{3,2,1,0:T(8,128)}, u32[]{:S(2)}, u32[]{:S(2)}) collective-permute-start(f32[4,1,64,128]{3,2,1,0:T(8,128)} %get-tuple-element.18), channel_id=1, source_target_pairs={{0,2},{2,4},{4,6},{6,8},{8,10},{10,12},{12,14},{14,16},{16,18},{18... | collective-permute-start | bytes 393224 | tf_op jit(solution)/shard_map/ppermute | solution.py:17
  19.3 5.6 %collective-permute-start.6 = (f32[2,8,128]{2,1,0:T(8,128)S(1)}, f32[2,8,128]{2,1,0:T(8,128)S(1)}, u32[]{:S(2)}, u32[]{:S(2)}) collective-permute-start(f32[2,8,128]{2,1,0:T(8,128)S(1)} %collective-permute-done.5), channel_id=1, source_target_pairs={{0,2},{2,4},{4,6},{6,8},{8,10},{10,12},{12,14},{14,16},{16,18},{18... | collective-permute-start | bytes 24584 | tf_op jit(solution)/shard_map/ppermute | solution.py:75
  20.6 4.9 %collective-permute-start.13 = (f32[2,8,128]{2,1,0:T(8,128)S(1)}, f32[2,8,128]{2,1,0:T(8,128)S(1)}, u32[]{:S(2)}, u32[]{:S(2)}) collective-permute-start(f32[2,8,128]{2,1,0:T(8,128)S(1)} %collective-permute-done.12), channel_id=1, source_target_pairs={{0,30},{2,0},{4,2},{6,4},{8,6},{10,8},{12,10},{14,12},{16,14},{18,... | collective-permute-start | bytes 24584 | tf_op jit(solution)/shard_map/ppermute | solution.py:77
  24.8 4.0 %collective-permute-start.7 = (f32[2,8,128]{2,1,0:T(8,128)S(1)}, f32[2,8,128]{2,1,0:T(8,128)S(1)}, u32[]{:S(2)}, u32[]{:S(2)}) collective-permute-start(f32[2,8,128]{2,1,0:T(8,128)S(1)} %collective-permute-done.6), channel_id=1, source_target_pairs={{0,2},{2,4},{4,6},{6,8},{8,10},{10,12},{12,14},{14,16},{16,18},{18... | collective-permute-start | bytes 24584 | tf_op jit(solution)/shard_map/ppermute | solution.py:75
  25.5 4.1 %collective-permute-start.14 = (f32[2,8,128]{2,1,0:T(8,128)S(1)}, f32[2,8,128]{2,1,0:T(8,128)S(1)}, u32[]{:S(2)}, u32[]{:S(2)}) collective-permute-start(f32[2,8,128]{2,1,0:T(8,128)S(1)} %collective-permute-done.13), channel_id=1, source_target_pairs={{0,30},{2,0},{4,2},{6,4},{8,6},{10,8},{12,10},{14,12},{16,14},{18,... | collective-permute-start | bytes 24584 | tf_op jit(solution)/shard_map/ppermute | solution.py:77
  28.8 4.0 %collective-permute-start.8 = (f32[2,8,128]{2,1,0:T(8,128)S(1)}, f32[2,8,128]{2,1,0:T(8,128)S(1)}, u32[]{:S(2)}, u32[]{:S(2)}) collective-permute-start(f32[2,8,128]{2,1,0:T(8,128)S(1)} %collective-permute-done.7), channel_id=1, source_target_pairs={{0,2},{2,4},{4,6},{6,8},{8,10},{10,12},{12,14},{14,16},{16,18},{18... | collective-permute-start | bytes 24584 | tf_op jit(solution)/shard_map/ppermute | solution.py:75
  29.6 4.9 %collective-permute-start.15 = (f32[2,8,128]{2,1,0:T(8,128)S(1)}, f32[2,8,128]{2,1,0:T(8,128)S(1)}, u32[]{:S(2)}, u32[]{:S(2)}) collective-permute-start(f32[2,8,128]{2,1,0:T(8,128)S(1)} %collective-permute-done.14), channel_id=1, source_target_pairs={{0,30},{2,0},{4,2},{6,4},{8,6},{10,8},{12,10},{14,12},{16,14},{18,... | collective-permute-start | bytes 24584 | tf_op jit(solution)/shard_map/ppermute | solution.py:77
  32.8 4.4 %collective-permute-start.9 = (f32[2,8,128]{2,1,0:T(8,128)S(1)}, f32[2,8,128]{2,1,0:T(8,128)S(1)}, u32[]{:S(2)}, u32[]{:S(2)}) collective-permute-start(f32[2,8,128]{2,1,0:T(8,128)S(1)} %collective-permute-done.8), channel_id=1, source_target_pairs={{0,2},{2,4},{4,6},{6,8},{8,10},{10,12},{12,14},{14,16},{16,18},{18... | collective-permute-start | bytes 24584 | tf_op jit(solution)/shard_map/ppermute | solution.py:75
  34.5 4.1 %collective-permute-start.16 = (f32[2,8,128]{2,1,0:T(8,128)S(1)}, f32[2,8,128]{2,1,0:T(8,128)}, u32[]{:S(2)}, u32[]{:S(2)}) collective-permute-start(f32[2,8,128]{2,1,0:T(8,128)S(1)} %collective-permute-done.15), channel_id=1, source_target_pairs={{0,30},{2,0},{4,2},{6,4},{8,6},{10,8},{12,10},{14,12},{16,14},{18,... | collective-permute-start | bytes 24584 | tf_op jit(solution)/shard_map/ppermute | solution.py:77
  37.2 4.1 %collective-permute-start.10 = (f32[2,8,128]{2,1,0:T(8,128)S(1)}, f32[2,8,128]{2,1,0:T(8,128)}, u32[]{:S(2)}, u32[]{:S(2)}) collective-permute-start(f32[2,8,128]{2,1,0:T(8,128)S(1)} %collective-permute-done.9), channel_id=1, source_target_pairs={{0,2},{2,4},{4,6},{6,8},{8,10},{10,12},{12,14},{14,16},{16,18},{18... | collective-permute-start | bytes 24584 | tf_op jit(solution)/shard_map/ppermute | solution.py:75
  38.6 4.3 %collective-permute-start.17 = (f32[2,8,128]{2,1,0:T(8,128)}, f32[2,8,128]{2,1,0:T(8,128)}, u32[]{:S(2)}, u32[]{:S(2)}) collective-permute-start(f32[2,8,128]{2,1,0:T(8,128)} %collective-permute-done.16), channel_id=1, source_target_pairs={{0,30},{2,0},{4,2},{6,4},{8,6},{10,8},{12,10},{14,12},{16,14},{18,... | collective-permute-start | bytes 24584 | tf_op jit(solution)/shard_map/ppermute | solution.py:77
  41.3 4.3 %collective-permute-start.11 = (f32[2,8,128]{2,1,0:T(8,128)}, f32[2,8,128]{2,1,0:T(8,128)}, u32[]{:S(2)}, u32[]{:S(2)}) collective-permute-start(f32[2,8,128]{2,1,0:T(8,128)} %collective-permute-done.10), channel_id=1, source_target_pairs={{0,2},{2,4},{4,6},{6,8},{8,10},{10,12},{12,14},{14,16},{16,18},{18... | collective-permute-start | bytes 24584 | tf_op jit(solution)/shard_map/ppermute | solution.py:75
  42.9 11.9 %collective-permute-start.18 = (f32[2,8,128]{2,1,0:T(8,128)}, f32[2,8,128]{2,1,0:T(8,128)S(1)}, u32[]{:S(2)}, u32[]{:S(2)}) collective-permute-start(f32[2,8,128]{2,1,0:T(8,128)} %collective-permute-done.17), channel_id=1, source_target_pairs={{0,30},{2,0},{4,2},{6,4},{8,6},{10,8},{12,10},{14,12},{16,14},{18,... | collective-permute-start | bytes 24584 | tf_op jit(solution)/shard_map/ppermute | solution.py:77
  63.9 6.6 %collective-permute-start.2 = (f32[4,4,1,128]{3,2,1,0:T(1,128)S(1)}, f32[4,4,1,128]{3,2,1,0:T(1,128)S(1)}, u32[]{:S(2)}, u32[]{:S(2)}) collective-permute-start(f32[4,4,1,128]{3,2,1,0:T(1,128)S(1)} %get-tuple-element.12), channel_id=1, source_target_pairs={{0,1},{2,3},{4,5},{6,7},{8,9},{10,11},{12,13},{14,15},{16,17},{18,... | collective-permute-start | bytes 24584 | tf_op jit(solution)/shard_map/ppermute | solution.py:17
  65.2 6.0 %collective-permute-start.3 = (f32[4,4,1,128]{3,2,1,0:T(1,128)S(1)}, f32[4,4,1,128]{3,2,1,0:T(1,128)S(1)}, u32[]{:S(2)}, u32[]{:S(2)}) collective-permute-start(f32[4,4,1,128]{3,2,1,0:T(1,128)S(1)} %get-tuple-element.13), channel_id=1, source_target_pairs={{1,0},{3,2},{5,4},{7,6},{9,8},{11,10},{13,12},{15,14},{17,16},{19,... | collective-permute-start | bytes 24584 | tf_op jit(solution)/shard_map/ppermute | solution.py:19
  188.1 5.1 %collective-permute-start.20 = (f32[4,1,64,128]{3,2,1,0:T(8,128)}, f32[4,1,64,128]{3,2,1,0:T(8,128)S(1)}, u32[]{:S(2)}, u32[]{:S(2)}) collective-permute-start(f32[4,1,64,128]{3,2,1,0:T(8,128)} %get-tuple-element.15), channel_id=1, source_target_pairs={{2,0},{4,2},{6,4},{8,6},{10,8},{12,10},{14,12},{16,14},{18,16},{20... | collective-permute-start | bytes 393224 | tf_op jit(solution)/shard_map/ppermute | solution.py:19
  190.0 7.5 %collective-permute-start.19 = (f32[4,1,64,128]{3,2,1,0:T(8,128)}, f32[4,1,64,128]{3,2,1,0:T(8,128)}, u32[]{:S(2)}, u32[]{:S(2)}) collective-permute-start(f32[4,1,64,128]{3,2,1,0:T(8,128)} %get-tuple-element.14), channel_id=1, source_target_pairs={{0,2},{2,4},{4,6},{6,8},{8,10},{10,12},{12,14},{14,16},{16,18},{18... | collective-permute-start | bytes 393224 | tf_op jit(solution)/shard_map/ppermute | solution.py:17
  198.3 4.4 %collective-permute-start.21 = (f32[4,4,1,128]{3,2,1,0:T(1,128)S(1)}, f32[4,4,1,128]{3,2,1,0:T(1,128)S(1)}, u32[]{:S(2)}, u32[]{:S(2)}) collective-permute-start(f32[4,4,1,128]{3,2,1,0:T(1,128)S(1)} %get-tuple-element.8), channel_id=1, source_target_pairs={{1,0},{3,2},{5,4},{7,6},{9,8},{11,10},{13,12},{15,14},{17,16},{19,... | collective-permute-start | bytes 24584 | tf_op jit(solution)/shard_map/ppermute | solution.py:19
  200.7 5.5 %collective-permute-start.22 = (f32[4,4,1,128]{3,2,1,0:T(1,128)S(1)}, f32[4,4,1,128]{3,2,1,0:T(1,128)S(1)}, u32[]{:S(2)}, u32[]{:S(2)}) collective-permute-start(f32[4,4,1,128]{3,2,1,0:T(1,128)S(1)} %get-tuple-element.9), channel_id=1, source_target_pairs={{0,1},{2,3},{4,5},{6,7},{8,9},{10,11},{12,13},{14,15},{16,17},{18,... | collective-permute-start | bytes 24584 | tf_op jit(solution)/shard_map/ppermute | solution.py:17
  (17 other events, 388.4 us)
Sparse Core Ops, SparseCore 0:
  84.7 97.3 all-reduce.1
